TPU v7x, 256 devices: a whole 4x4x8 slice. The times are simulated.
256 devices in a mesh: req: 8 (over z), seq: 32 (over y, x, core).
Axes of the slice: x: 4, y: 4, z: 8, core: 2. Of those that a mesh axis runs over, the one named last changes fastest.
Arguments:
- hidden_in: bfloat16 [16, 1024, 2048], P('req', 'seq'), may hold values from -6 to 6
- norm_gain: float32 [2048], replicated, may hold values from 0.1 to 1.9
- w_query: bfloat16 [2048, 1024], P(('req', 'seq')), may hold values from -0.125 to 0.125
- w_key: bfloat16 [2048, 512], P(('req', 'seq')), may hold values from -0.3125 to 0.3125
- w_value: bfloat16 [2048, 512], P(('req', 'seq')), may hold values from -0.125 to 0.125
- cache_keys: bfloat16 [16, 8192, 512], P('req', 'seq'), may hold values from -525 to 525
- cache_values: bfloat16 [16, 8192, 512], P('req', 'seq'), may hold values from -6 to 6
- cache_lengths: int32 [16], P('req'), may hold values from 1 to 8192, as said below
Outputs:
- attended: bfloat16 [16, 1024, 1024], P('req', 'seq')
- new_keys: bfloat16 [16, 1024, 512], P('req', 'seq')
- new_values: bfloat16 [16, 1024, 512], P('req', 'seq')
Inputs may be any that keep to these rules, and one draw needn't show every extreme that they name: `cache_lengths`: some request's cache holds exactly 8192 positions.
All inputs are finite; a program needn't handle non-finite values.
Results may differ from a plain program's by a relative error of at most 0.034.
Values may be sent and summed in bfloat16 or wider, within the bound.
No kernel may reach another device: no remote copies, remote signals or barrier semaphores. Data moves between devices by JAX's collectives and lax.ppermute only.
A program may use at most 128 MiB of HBM per device.

v0:
```python
import jax
import jax.numpy as jnp
from jax import lax
from jax.sharding import PartitionSpec as P

HEADS = 4
KV_HEADS = 2
HEAD = 256
EPSILON = 1e-06
THETA = 1000042.0
MASKED = -1e30


def tables(positions, head_size):
    half_size = head_size // 2
    frequency = THETA ** (-(jnp.arange(half_size, dtype=jnp.float32) * 2.0 / head_size))
    angles = positions.astype(jnp.float32)[..., None] * frequency
    return (jnp.cos(angles)[..., None, :], jnp.sin(angles)[..., None, :])


def rotate(values, cosine, sine_part):
    half_size = values.shape[-1] // 2
    first_half = values[..., :half_size]
    second_half = values[..., half_size:]
    return jnp.concatenate(
        [
            first_half * cosine - second_half * sine_part,
            second_half * cosine + first_half * sine_part,
        ],
        axis=-1,
    )


def attend(query_rows, key_rows, value_rows, live):
    span_len = query_rows.shape[0]
    group_size = HEADS // KV_HEADS
    query_view = query_rows.reshape(span_len, KV_HEADS, group_size, HEAD)
    key_view = key_rows.reshape(key_rows.shape[0], KV_HEADS, HEAD)
    value_view = value_rows.reshape(value_rows.shape[0], KV_HEADS, HEAD)
    scores = jnp.einsum(
        "cgeh,kgh->cgek", query_view, key_view, preferred_element_type=jnp.float32
    ) * HEAD ** (-0.5)
    mask_view = live[:, None, None, :]
    scores = jnp.where(mask_view, scores, MASKED)
    block_max = jnp.max(scores, axis=-1)
    weights = jnp.where(mask_view, jnp.exp(scores - block_max[..., None]), 0.0)
    block_sum = jnp.sum(weights, axis=-1)
    block_out = jnp.einsum(
        "cgek,kgh->cgeh",
        weights.astype(jnp.bfloat16),
        value_view,
        preferred_element_type=jnp.float32,
    )
    return (
        block_max.reshape(span_len, HEADS),
        block_sum.reshape(span_len, HEADS),
        block_out.reshape(span_len, HEADS * HEAD).astype(jnp.bfloat16),
    )


def attend_rows(query_rows, key_rows, value_rows, live):
    total_rows = query_rows.shape[0]
    row_block = min(512, total_rows)
    pieces = []
    for begin in range(0, total_rows, row_block):
        pieces.append(
            attend(
                query_rows[begin : begin + row_block],
                key_rows,
                value_rows,
                live[begin : begin + row_block],
            )
        )
    return tuple((jnp.concatenate([piece[slot] for piece in pieces], axis=0) for slot in range(3)))


def body(hidden_in, norm_gain, w_query, w_key, w_value, cache_keys, cache_values, cache_lengths):
    seq_count = lax.axis_size("seq")
    seq_seat = lax.axis_index("seq")
    req_local, slice_len, model_width = hidden_in.shape
    cache_len_dev = cache_keys.shape[1]
    span_len = slice_len * seq_count
    inputs = hidden_in.astype(jnp.float32)
    normed = (
        inputs * lax.rsqrt(jnp.mean(inputs * inputs, axis=-1, keepdims=True) + EPSILON) * norm_gain
    ).astype(jnp.bfloat16)
    flat_rows = normed.reshape(req_local * slice_len, model_width)
    full_query, full_key, full_value = (
        lax.all_gather(w_query, ("req", "seq"), axis=0, tiled=True),
        lax.all_gather(w_key, ("req", "seq"), axis=0, tiled=True),
        lax.all_gather(w_value, ("req", "seq"), axis=0, tiled=True),
    )
    query_raw = jnp.dot(flat_rows, full_query, preferred_element_type=jnp.float32)
    key_raw = jnp.dot(flat_rows, full_key, preferred_element_type=jnp.float32)
    value_raw = jnp.dot(flat_rows, full_value, preferred_element_type=jnp.float32)
    local_index = jnp.arange(slice_len, dtype=jnp.int32)
    positions = cache_lengths[:, None] + seq_seat * slice_len + local_index[None, :]
    cosine, sine_part = tables(positions, HEAD)
    queries = (
        rotate(query_raw.reshape(req_local, slice_len, HEADS, HEAD), cosine, sine_part)
        .reshape(req_local, slice_len, HEADS * HEAD)
        .astype(jnp.bfloat16)
    )
    new_keys = (
        rotate(key_raw.reshape(req_local, slice_len, KV_HEADS, HEAD), cosine, sine_part)
        .reshape(req_local, slice_len, KV_HEADS * HEAD)
        .astype(jnp.bfloat16)
    )
    new_values = value_raw.reshape(req_local, slice_len, KV_HEADS * HEAD).astype(jnp.bfloat16)
    all_queries = lax.all_gather(queries, "seq", axis=1, tiled=True)
    key_block = jnp.concatenate([cache_keys, new_keys], axis=1)
    value_block = jnp.concatenate([cache_values, new_values], axis=1)
    span_index = jnp.arange(span_len, dtype=jnp.int32)
    cache_pos = seq_seat * cache_len_dev + jnp.arange(cache_len_dev, dtype=jnp.int32)
    new_pos = seq_seat * slice_len + local_index
    new_live = new_pos[None, :] <= span_index[:, None]
    max_list = []
    sum_list = []
    out_list = []
    for request in range(req_local):
        cache_live = cache_pos < cache_lengths[request]
        live_full = jnp.concatenate(
            [jnp.broadcast_to(cache_live[None, :], (span_len, cache_len_dev)), new_live], axis=1
        )
        query_rows = all_queries[request]
        terms = attend_rows(query_rows, key_block[request], value_block[request], live_full)
        max_list.append(terms[0])
        sum_list.append(terms[1])
        out_list.append(terms[2])
    max_all = jnp.stack(max_list)
    sum_all = jnp.stack(sum_list)
    out_all = jnp.stack(out_list)
    got_max, got_sum = (
        lax.all_to_all(max_all, "seq", split_axis=1, concat_axis=0, tiled=True),
        lax.all_to_all(sum_all, "seq", split_axis=1, concat_axis=0, tiled=True),
    )
    got_out = lax.all_to_all(out_all, "seq", split_axis=1, concat_axis=0, tiled=True)
    got_max = got_max.reshape(seq_count, req_local, slice_len, HEADS)
    got_sum = got_sum.reshape(seq_count, req_local, slice_len, HEADS)
    got_out = got_out.reshape(seq_count, req_local, slice_len, HEADS, HEAD)
    best_max = jnp.max(got_max, axis=0)
    factor = jnp.exp(got_max - best_max)
    total_sum = jnp.sum(got_sum * factor, axis=0)
    total_out = jnp.sum(got_out.astype(jnp.float32) * factor[..., None], axis=0)
    attended = (
        (total_out / total_sum[..., None])
        .reshape(req_local, slice_len, HEADS * HEAD)
        .astype(jnp.bfloat16)
    )
    return (attended, new_keys, new_values)


def solution(mesh):
    in_specs = (
        P("req", "seq", None),
        P(),
        P(("req", "seq"), None),
        P(("req", "seq"), None),
        P(("req", "seq"), None),
        P("req", "seq", None),
        P("req", "seq", None),
        P("req"),
    )
    out_specs = (P("req", "seq", None), P("req", "seq", None), P("req", "seq", None))
    return jax.shard_map(body, mesh=mesh, in_specs=in_specs, out_specs=out_specs, check_vma=False)
```

profile of v0, /device:TPU:32, one launch (start us, length us, event | category | flops | bytes accessed | tf_op | source)
XLA Modules:
  0.0 553.0 jit_solution(8246084704090221894)
XLA Ops:
  11.5 117.5 %all-gather.9.cloned.1.call-done = bf16[2048,1024]{1,0:T(8,128)(2,1)} async-done(((bf16[8,1024]{1,0:T(8,128)(2,1)}), bf16[2048,1024]{1,0:T(8,128)(2,1)}) %all-gather.9.cloned.1.call-update) | async-done | bytes 4194320 | tf_op jit(solution)/shard_map/all_gather | solution.py:89
  129.0 6.6 %copy.99 = bf16[1024,2048]{1,0:T(8,128)(2,1)} copy(bf16[1024,2048]{0,1:T(8,128)(2,1)} %bitcast.163) | data formatting | bytes 8388608 | tf_op jit(solution)/shard_map/dot_general | solution.py:93
  135.6 3.6 fusion.47
  143.7 91.3 %all-gather.7.cloned.1.call-done = bf16[2048,512]{1,0:T(8,128)(2,1)} async-done(((bf16[8,512]{1,0:T(8,128)(2,1)}), bf16[2048,512]{1,0:T(8,128)(2,1)}) %all-gather.7.cloned.1.call-update) | async-done | bytes 2097168 | tf_op jit(solution)/shard_map/all_gather | solution.py:90
  235.0 2.9 copy.97
  239.7 102.3 %all-gather.5.cloned.1.call-done = bf16[2048,512]{1,0:T(8,128)(2,1)} async-done(((bf16[8,512]{1,0:T(8,128)(2,1)}), bf16[2048,512]{1,0:T(8,128)(2,1)}) %all-gather.5.cloned.1.call-update) | async-done | bytes 2097168 | tf_op jit(solution)/shard_map/all_gather | solution.py:91
  342.0 2.1 fusion.40
  346.5 48.8 %all-gather.11.cloned.1.call-done = bf16[2,1024,1024]{2,1,0:T(8,128)(2,1)} async-done(((bf16[2,32,1024]{2,1,0:T(8,128)(2,1)}), bf16[2,1024,1024]{2,1,0:T(8,128)(2,1)}) %all-gather.11.cloned.1.call-update) | async-done | bytes 4194320 | tf_op jit(solution)/shard_map/all_gather | solution.py:110
  395.3 3.9 fusion.87
  399.1 2.3 copy.101
  401.4 3.3 fusion.4
  405.3 3.0 fusion.8
  408.4 3.1 convolution_convert_fusion.3
  412.8 3.4 fusion.5
  416.7 3.9 convolution_convert_fusion.2
  423.1 2.5 fusion.6
  426.9 2.2 fusion.12
  429.1 2.1 convolution_convert_fusion.1
  432.0 2.2 fusion.7
  435.4 3.1 convolution_convert_fusion
  445.7 2.1 reshape.179
  447.8 5.2 all-to-all-start.1
  454.9 3.1 maximum_bitcast_fusion.1
  459.2 3.3 reshape.181
  462.6 7.4 %all-to-all-start.2 = ((f32[32,1,256]{2,1,0:T(1,128)}), f32[32,1,256]{2,1,0:T(1,128)S(1)}, u32[]{:S(2)}, u32[]{:S(2)}) async-start(f32[32,1,256]{2,1,0:T(1,128)} %reshape.181), calls=%async_computation.2 | async-start | bytes 65536 | tf_op jit(solution)/shard_map/all_to_all | solution.py:135
  470.0 2.0 pad_maximum_fusion
  471.9 6.3 %copy.121 = bf16[2,1024,1024]{2,0,1:T(2,128)(2,1)} copy(bf16[2,1024,1024]{2,1,0:T(8,128)(2,1)S(1)} %pad_maximum_fusion) | data formatting | bytes 8388608 | tf_op jit(solution)/shard_map/stack | solution.py:132
  478.2 7.7 %all-to-all-start = ((bf16[2,1024,1024]{2,0,1:T(2,128)(2,1)}), bf16[2,1024,1024]{2,0,1:T(2,128)(2,1)}, u32[]{:S(2)}, u32[]{:S(2)}) async-start(bf16[2,1024,1024]{2,0,1:T(2,128)(2,1)} %copy.121), calls=%async_computation | async-start | bytes 8388608 | tf_op jit(solution)/shard_map/all_to_all | solution.py:137
  493.3 4.5 mul.173
  497.9 10.8 %mul.174 = f32[32,2,32,1024]{3,2,0,1:T(8,128)} reshape(f32[32,2,32,4,256]{4,3,2,0,1:T(4,128)} %mul.173) | data formatting | bytes 16777216 | tf_op jit(solution)/shard_map/mul | solution.py:144
  509.0 30.7 %all-to-all-done = bf16[2,1024,1024]{2,0,1:T(2,128)(2,1)} async-done(((bf16[2,1024,1024]{2,0,1:T(2,128)(2,1)}), bf16[2,1024,1024]{2,0,1:T(2,128)(2,1)}, u32[]{:S(2)}, u32[]{:S(2)}) %all-to-all-start) | async-done | bytes 4194336 | tf_op jit(solution)/shard_map/all_to_all | solution.py:137
  539.7 3.7 copy.122
  (136 shorter events, 42.0 us)
Async XLA Ops:
  7.2 121.8 %all-gather.9.cloned.1.call-start = ((), (), s32[]{:S(2)}) async-start(), calls=%async_computation.5 | async-start | bytes 4210688 | tf_op jit(solution)/shard_map/all_gather | solution.py:89
  7.9 227.1 %all-gather.7.cloned.1.call-start = ((), (), s32[]{:S(2)}) async-start(), calls=%async_computation.4 | async-start | bytes 2105344 | tf_op jit(solution)/shard_map/all_gather | solution.py:90
  8.6 333.3 %all-gather.5.cloned.1.call-start = ((), (), s32[]{:S(2)}) async-start(), calls=%async_computation.3 | async-start | bytes 2105344 | tf_op jit(solution)/shard_map/all_gather | solution.py:91
  9.4 385.9 %all-gather.11.cloned.1.call-start = ((), (), s32[]{:S(2)}) async-start(), calls=%async_computation.6 | async-start | bytes 4325376 | tf_op jit(solution)/shard_map/all_gather | solution.py:110
  129.0 6.6 %copy-start.1 = (bf16[2,32,2048]{2,1,0:T(8,128)(2,1)S(1)}, bf16[2,32,2048]{2,1,0:T(8,128)(2,1)}, u32[]{:S(2)}) copy-start(bf16[2,32,2048]{2,1,0:T(8,128)(2,1)} %param.8) | copy-start | bytes 786436
  129.0 6.6 %copy-start.16 = (f32[2048]{0:T(1024)S(1)}, f32[2048]{0:T(1024)}, u32[]{:S(2)}) copy-start(f32[2048]{0:T(1024)} %param.9) | copy-start | bytes 24580
  135.6 4.4 copy-start.27
  135.6 6.4 %copy-start.10 = (bf16[2,256,512]{2,1,0:T(8,128)(2,1)S(1)}, bf16[2,256,512]{2,1,0:T(8,128)(2,1)}, u32[]{:S(2)}) copy-start(bf16[2,256,512]{2,1,0:T(8,128)(2,1)} %param.13) | copy-start | bytes 1572868
  238.8 105.3 %copy-start.11 = (bf16[2,256,512]{2,1,0:T(8,128)(2,1)S(1)}, bf16[2,256,512]{2,1,0:T(8,128)(2,1)}, u32[]{:S(2)}) copy-start(bf16[2,256,512]{2,1,0:T(8,128)(2,1)} %param.14) | copy-start | bytes 1572868
  344.1 55.0 %copy-start.14 = (bf16[2,32,512]{2,1,0:T(8,128)(2,1)}, bf16[2,32,512]{2,1,0:T(8,128)(2,1)S(1)}, u32[]{:S(2)}) copy-start(bf16[2,32,512]{2,1,0:T(8,128)(2,1)S(1)} %fusion.40) | copy-start | bytes 196612
  405.3 3.0 copy-start.3
  405.3 3.0 copy-start.9
  412.8 4.0 copy-start.13
  416.7 3.9 copy-start.2
  426.9 2.2 copy-start.8
  426.9 2.2 copy-start.12
  426.9 2.2 copy-start.22
  435.4 3.1 copy-start.21
  439.7 2.7 copy-start.6
  441.0 2.7 copy-start.7
  442.4 2.7 copy-start.23
  442.4 2.7 copy-start.24
  442.4 2.7 copy-start.25
  442.4 2.7 copy-start.26
  443.7 9.3 %copy-start.17 = (f32[512,2,2]{0,2,1:T(2,128)S(1)}, f32[512,2,2]{0,2,1:T(2,128)}, u32[]{:S(2)}) copy-start(f32[512,2,2]{0,2,1:T(2,128)} %fusion.8) | copy-start | bytes 24580
  443.7 9.4 %copy-start.18 = (f32[512,2,2]{0,2,1:T(2,128)S(1)}, f32[512,2,2]{0,2,1:T(2,128)}, u32[]{:S(2)}) copy-start(f32[512,2,2]{0,2,1:T(2,128)} %fusion.10) | copy-start | bytes 24580
  443.7 9.4 %copy-start.19 = (f32[512,2,2]{0,2,1:T(2,128)S(1)}, f32[512,2,2]{0,2,1:T(2,128)}, u32[]{:S(2)}) copy-start(f32[512,2,2]{0,2,1:T(2,128)} %fusion.12) | copy-start | bytes 24580
  443.7 9.4 %copy-start.20 = (f32[512,2,2]{0,2,1:T(2,128)S(1)}, f32[512,2,2]{0,2,1:T(2,128)}, u32[]{:S(2)}) copy-start(f32[512,2,2]{0,2,1:T(2,128)} %fusion.14) | copy-start | bytes 24580
  447.8 14.8 %all-to-all-start.1 = ((f32[32,1,256]{2,1,0:T(1,128)}), f32[32,1,256]{2,1,0:T(1,128)S(1)}, u32[]{:S(2)}, u32[]{:S(2)}) async-start(f32[32,1,256]{2,1,0:T(1,128)} %reshape.179), calls=%async_computation.1 | async-start | bytes 65536 | tf_op jit(solution)/shard_map/all_to_all | solution.py:134
  462.6 15.7 %all-to-all-start.2 = ((f32[32,1,256]{2,1,0:T(1,128)}), f32[32,1,256]{2,1,0:T(1,128)S(1)}, u32[]{:S(2)}, u32[]{:S(2)}) async-start(f32[32,1,256]{2,1,0:T(1,128)} %reshape.181), calls=%async_computation.2 | async-start | bytes 65536 | tf_op jit(solution)/shard_map/all_to_all | solution.py:135
  478.2 61.5 %all-to-all-start = ((bf16[2,1024,1024]{2,0,1:T(2,128)(2,1)}), bf16[2,1024,1024]{2,0,1:T(2,128)(2,1)}, u32[]{:S(2)}, u32[]{:S(2)}) async-start(bf16[2,1024,1024]{2,0,1:T(2,128)(2,1)} %copy.121), calls=%async_computation | async-start | bytes 8388608 | tf_op jit(solution)/shard_map/all_to_all | solution.py:137
  539.7 4.6 copy-start
  (3 other events, 3.4 us)
Sparse Core Ops, SparseCore 0:
  11.6 117.4 all-gather.8
  132.7 102.2 all-gather.6
  238.8 103.1 all-gather.4
  345.0 50.2 all-gather.10
where the time goes:
time: 554 us; the launch traced here: 553 us
  waiting for transfers between devices  393 us (71%)
  local copies, waits for them, and re-layouts  73.6 us (13%)
  matrix products  30 us (5%)
  other arithmetic  22 us (4%)
  starting transfers between devices  20.5 us (4%)
  between operations  14.2 us (3%)
    all_gather x1, waiting for transfers between devices, body(): lax.all_gather(w_query, ('req', 'seq'), axis=0, tiled=True)  118 us
    all_gather x1, waiting for transfers between devices, body(): lax.all_gather(w_value, ('req', 'seq'), axis=0, tiled=True)  102 us
    all_gather x1, waiting for transfers between devices, body(): lax.all_gather(w_key, ('req', 'seq'), axis=0, tiled=True)  91.3 us
    all_gather x1, waiting for transfers between devices, body(): all_queries = lax.all_gather(queries, 'seq', axis=1, tiled=True)  48.8 us
    all_to_all x1, waiting for transfers between devices, body(): lax.all_to_all(out_all, 'seq', split_axis=1, concat_axis=0, tiled=True)  30.7 us
    mul x2, local copies, waits for them, and re-layouts, body(): total_out = jnp.sum(got_out.astype(jnp.float32) * factor[..., None], axis=0)  15.3 us
    dot_general x4, matrix products, attend(): jnp.einsum('cgek,kgh->cgeh', weights.astype(jnp.bfloat16), value_view, pr...  12.1 us
    dot_general x4, matrix products, attend(): jnp.einsum('cgeh,kgh->cgek', query_view, key_view, preferred_element_type...  11.4 us
  transfers between devices with their start and end apart: 7, of which 5 were waited for; matrix products, arithmetic and copies ran while one was open for 12% of the time, Pallas kernels for 0%

commit v1 on v0

--- a/solution.py
+++ b/solution.py
@@ -88,7 +88,12 @@
     full_query, full_key, full_value = (
         lax.all_gather(w_query, ("req", "seq"), axis=0, tiled=True),
         lax.all_gather(w_key, ("req", "seq"), axis=0, tiled=True),
-        lax.all_gather(w_value, ("req", "seq"), axis=0, tiled=True),
+        jnp.concatenate(
+            lax.all_to_all(
+                jnp.stack([w_value] * lax.axis_size(("req", "seq"))), ("req", "seq"), 0, 0
+            ),
+            axis=0,
+        ),
     )
     query_raw = jnp.dot(flat_rows, full_query, preferred_element_type=jnp.float32)
     key_raw = jnp.dot(flat_rows, full_key, preferred_element_type=jnp.float32)

time: 554 us -> 451 us (0.81)
  waiting for transfers between devices: 393 us -> 275 us
  starting transfers between devices: 20.5 us -> 30.7 us
    all_gather x1 -> x0, waiting for transfers between devices: 102 us -> none  [body(): lax.all_gather(w_value, ('req', 'seq'), axis=0, tiled=True)]
    all_to_all x0 -> x1, starting transfers between devices: none -> 10.1 us  [body(): lax.all_to_all(jnp.stack([w_value] * lax.axis_size(('req', 'seq'))), ('re...]
    all_gather x1, waiting for transfers between devices: 91.3 us -> 83.4 us  [body(): lax.all_gather(w_key, ('req', 'seq'), axis=0, tiled=True)]
    all_gather x1, waiting for transfers between devices: 48.8 us -> 41.6 us  [body(): all_queries = lax.all_gather(queries, 'seq', axis=1, tiled=True)]
  transfers between devices with their start and end apart: 7 -> 7, of which waited for: 5 -> 4; matrix products, arithmetic and copies ran while one was open for 12% -> 16% of each run, Pallas kernels for 0% -> 0%
where the time goes in v1:
time: 451 us; the launch traced here: 450 us
  waiting for transfers between devices  275 us (61%)
  local copies, waits for them, and re-layouts  77 us (17%)
  starting transfers between devices  30.7 us (7%)
  matrix products  30 us (7%)
  other arithmetic  22.8 us (5%)
  between operations  14.2 us (3%)
    all_gather x1, waiting for transfers between devices, body(): lax.all_gather(w_query, ('req', 'seq'), axis=0, tiled=True)  118 us
    all_gather x1, waiting for transfers between devices, body(): lax.all_gather(w_key, ('req', 'seq'), axis=0, tiled=True)  83.4 us
    all_gather x1, waiting for transfers between devices, body(): all_queries = lax.all_gather(queries, 'seq', axis=1, tiled=True)  41.6 us
    all_to_all x1, waiting for transfers between devices, body(): lax.all_to_all(out_all, 'seq', split_axis=1, concat_axis=0, tiled=True)  30.6 us
    mul x2, local copies, waits for them, and re-layouts, body(): total_out = jnp.sum(got_out.astype(jnp.float32) * factor[..., None], axis=0)  15.4 us
    dot_general x4, matrix products, attend(): jnp.einsum('cgek,kgh->cgeh', weights.astype(jnp.bfloat16), value_view, pr...  12.1 us
    dot_general x4, matrix products, attend(): jnp.einsum('cgeh,kgh->cgek', query_view, key_view, preferred_element_type...  11.5 us
    unnamed x67, local copies, waits for them, and re-layouts  10.5 us
  transfers between devices with their start and end apart: 7, of which 4 were waited for; matrix products, arithmetic and copies ran while one was open for 16% of the time, Pallas kernels for 0%

profile of v1, /device:TPU:32, one launch (start us, length us, event | category | flops | bytes accessed | tf_op | source)
XLA Modules:
  0.0 449.9 jit_solution(4956256277310240169)
XLA Ops:
  10.7 118.3 %all-gather.6.cloned.1.call-done = bf16[2048,1024]{1,0:T(8,128)(2,1)} async-done(((bf16[8,1024]{1,0:T(8,128)(2,1)}), bf16[2048,1024]{1,0:T(8,128)(2,1)}) %all-gather.6.cloned.1.call-update) | async-done | bytes 4194320 | tf_op jit(solution)/shard_map/all_gather | solution.py:89
  129.0 6.6 %copy.99 = bf16[1024,2048]{1,0:T(8,128)(2,1)} copy(bf16[1024,2048]{0,1:T(8,128)(2,1)} %bitcast.165) | data formatting | bytes 8388608 | tf_op jit(solution)/shard_map/dot_general | solution.py:98
  135.6 3.6 fusion.47
  141.5 10.1 %all-to-all-start = ((bf16[256,8,512]{2,1,0:T(8,128)(2,1)}), bf16[256,8,512]{2,1,0:T(8,128)(2,1)S(1)}, u32[]{:S(2)}, u32[]{:S(2)}) async-start(bf16[256,8,512]{2,1,0:T(8,128)(2,1)} %stack.20), calls=%async_computation | async-start | bytes 4194304 | tf_op jit(solution)/shard_map/all_to_all | solution.py:92
  155.4 83.4 %all-gather.4.cloned.1.call-done = bf16[2048,512]{1,0:T(8,128)(2,1)} async-done(((bf16[8,512]{1,0:T(8,128)(2,1)}), bf16[2048,512]{1,0:T(8,128)(2,1)}) %all-gather.4.cloned.1.call-update) | async-done | bytes 2097168 | tf_op jit(solution)/shard_map/all_gather | solution.py:90
  238.8 4.0 copy.97
  242.8 2.3 fusion.49
  250.7 41.6 %all-gather.8.cloned.1.call-done = bf16[2,1024,1024]{2,1,0:T(8,128)(2,1)} async-done(((bf16[2,32,1024]{2,1,0:T(8,128)(2,1)}), bf16[2,1024,1024]{2,1,0:T(8,128)(2,1)}) %all-gather.8.cloned.1.call-update) | async-done | bytes 4194320 | tf_op jit(solution)/shard_map/all_gather | solution.py:115
  292.2 3.9 fusion.87
  296.1 2.3 copy.101
  298.4 3.4 fusion.4
  302.4 3.0 fusion.8
  305.4 3.1 convolution_convert_fusion.3
  309.8 3.4 fusion.5
  313.8 3.9 convolution_convert_fusion.2
  320.2 2.5 fusion.6
  324.0 2.0 fusion.12
  326.0 2.1 convolution_convert_fusion.1
  328.9 2.2 fusion.7
  332.4 3.0 convolution_convert_fusion
  342.6 2.1 reshape.185
  344.7 5.3 %all-to-all-start.2 = ((f32[32,1,256]{2,1,0:T(1,128)}), f32[32,1,256]{2,1,0:T(1,128)S(1)}, u32[]{:S(2)}, u32[]{:S(2)}) async-start(f32[32,1,256]{2,1,0:T(1,128)} %reshape.185), calls=%async_computation.2 | async-start | bytes 65536 | tf_op jit(solution)/shard_map/all_to_all | solution.py:139
  351.8 3.0 maximum_bitcast_fusion.1
  356.2 3.3 reshape.187
  359.5 7.6 %all-to-all-start.3 = ((f32[32,1,256]{2,1,0:T(1,128)}), f32[32,1,256]{2,1,0:T(1,128)S(1)}, u32[]{:S(2)}, u32[]{:S(2)}) async-start(f32[32,1,256]{2,1,0:T(1,128)} %reshape.187), calls=%async_computation.3 | async-start | bytes 65536 | tf_op jit(solution)/shard_map/all_to_all | solution.py:140
  367.2 2.0 pad_maximum_fusion
  369.1 6.3 %copy.121 = bf16[2,1024,1024]{2,0,1:T(2,128)(2,1)} copy(bf16[2,1024,1024]{2,1,0:T(8,128)(2,1)S(1)} %pad_maximum_fusion) | data formatting | bytes 8388608 | tf_op jit(solution)/shard_map/stack | solution.py:137
  375.5 7.6 %all-to-all-start.1 = ((bf16[2,1024,1024]{2,0,1:T(2,128)(2,1)}), bf16[2,1024,1024]{2,0,1:T(2,128)(2,1)}, u32[]{:S(2)}, u32[]{:S(2)}) async-start(bf16[2,1024,1024]{2,0,1:T(2,128)(2,1)} %copy.121), calls=%async_computation.1 | async-start | bytes 8388608 | tf_op jit(solution)/shard_map/all_to_all | solution.py:142
  390.4 4.6 %mul.173 = f32[32,2,32,4,256]{4,3,2,0,1:T(4,128)} broadcast(f32[32,2,32,4]{3,2,0,1:T(8,128)S(1)} %copy.125), dimensions={0,1,2,3} | broadcast | bytes 8421376 | tf_op jit(solution)/shard_map/mul | solution.py:149
  394.9 10.8 %mul.174 = f32[32,2,32,1024]{3,2,0,1:T(8,128)} reshape(f32[32,2,32,4,256]{4,3,2,0,1:T(4,128)} %mul.173) | data formatting | bytes 16777216 | tf_op jit(solution)/shard_map/mul | solution.py:149
  406.1 30.6 %all-to-all-done.1 = bf16[2,1024,1024]{2,0,1:T(2,128)(2,1)} async-done(((bf16[2,1024,1024]{2,0,1:T(2,128)(2,1)}), bf16[2,1024,1024]{2,0,1:T(2,128)(2,1)}, u32[]{:S(2)}, u32[]{:S(2)}) %all-to-all-start.1) | async-done | bytes 4194336 | tf_op jit(solution)/shard_map/all_to_all | solution.py:142
  436.7 3.7 copy.122
  (142 shorter events, 44.4 us)
Async XLA Ops:
  7.2 121.8 %all-gather.6.cloned.1.call-start = ((), (), s32[]{:S(2)}) async-start(), calls=%async_computation.5 | async-start | bytes 4210688 | tf_op jit(solution)/shard_map/all_gather | solution.py:89
  7.9 230.9 %all-gather.4.cloned.1.call-start = ((), (), s32[]{:S(2)}) async-start(), calls=%async_computation.4 | async-start | bytes 2105344 | tf_op jit(solution)/shard_map/all_gather | solution.py:90
  8.6 283.6 %all-gather.8.cloned.1.call-start = ((), (), s32[]{:S(2)}) async-start(), calls=%async_computation.6 | async-start | bytes 4325376 | tf_op jit(solution)/shard_map/all_gather | solution.py:115
  129.0 6.6 %copy-start.1 = (bf16[2,32,2048]{2,1,0:T(8,128)(2,1)S(1)}, bf16[2,32,2048]{2,1,0:T(8,128)(2,1)}, u32[]{:S(2)}) copy-start(bf16[2,32,2048]{2,1,0:T(8,128)(2,1)} %param.8) | copy-start | bytes 786436
  129.0 6.6 %copy-start.18 = (f32[2048]{0:T(1024)S(1)}, f32[2048]{0:T(1024)}, u32[]{:S(2)}) copy-start(f32[2048]{0:T(1024)} %param.9) | copy-start | bytes 24580
  135.6 4.4 copy-start.29
  141.5 10.1 %copy-start.30 = (s32[2]{0:T(128)S(1)}, s32[2]{0:T(128)}, u32[]{:S(2)}) copy-start(s32[2]{0:T(128)} %param.15) | copy-start | bytes 28
  141.5 12.1 %copy-start.13 = (bf16[2,256,512]{2,1,0:T(8,128)(2,1)S(1)}, bf16[2,256,512]{2,1,0:T(8,128)(2,1)}, u32[]{:S(2)}) copy-start(bf16[2,256,512]{2,1,0:T(8,128)(2,1)} %param.13) | copy-start | bytes 1572868
  141.5 105.2 %all-to-all-start = ((bf16[256,8,512]{2,1,0:T(8,128)(2,1)}), bf16[256,8,512]{2,1,0:T(8,128)(2,1)S(1)}, u32[]{:S(2)}, u32[]{:S(2)}) async-start(bf16[256,8,512]{2,1,0:T(8,128)(2,1)} %stack.20), calls=%async_computation | async-start | bytes 4194304 | tf_op jit(solution)/shard_map/all_to_all | solution.py:92
  247.2 3.5 copy-start.16
  250.7 47.7 %copy-start.12 = (pred[512,288]{0,1:T(8,128)(4,1)S(1)}, pred[512,288]{0,1:T(8,128)(4,1)}, u32[]{:S(2)}) copy-start(pred[512,288]{0,1:T(8,128)(4,1)} %get-tuple-element.13) | copy-start | bytes 442372
  302.4 3.0 copy-start.3
  305.4 4.4 copy-start.11
  309.8 4.0 copy-start.15
  313.8 3.9 copy-start.2
  317.7 2.5 copy-start.9
  326.0 2.9 copy-start.8
  332.4 3.0 copy-start.23
  336.6 2.7 copy-start.6
  337.9 2.7 copy-start.7
  339.3 2.7 copy-start.25
  339.3 2.7 copy-start.26
  339.3 2.7 copy-start.27
  339.3 2.7 copy-start.28
  340.6 9.4 %copy-start.19 = (f32[512,2,2]{0,2,1:T(2,128)S(1)}, f32[512,2,2]{0,2,1:T(2,128)}, u32[]{:S(2)}) copy-start(f32[512,2,2]{0,2,1:T(2,128)} %fusion.8) | copy-start | bytes 24580
  340.6 9.4 %copy-start.20 = (f32[512,2,2]{0,2,1:T(2,128)S(1)}, f32[512,2,2]{0,2,1:T(2,128)}, u32[]{:S(2)}) copy-start(f32[512,2,2]{0,2,1:T(2,128)} %fusion.10) | copy-start | bytes 24580
  340.6 9.4 %copy-start.21 = (f32[512,2,2]{0,2,1:T(2,128)S(1)}, f32[512,2,2]{0,2,1:T(2,128)}, u32[]{:S(2)}) copy-start(f32[512,2,2]{0,2,1:T(2,128)} %fusion.12) | copy-start | bytes 24580
  340.6 9.4 %copy-start.22 = (f32[512,2,2]{0,2,1:T(2,128)S(1)}, f32[512,2,2]{0,2,1:T(2,128)}, u32[]{:S(2)}) copy-start(f32[512,2,2]{0,2,1:T(2,128)} %fusion.14) | copy-start | bytes 24580
  344.7 14.8 %all-to-all-start.2 = ((f32[32,1,256]{2,1,0:T(1,128)}), f32[32,1,256]{2,1,0:T(1,128)S(1)}, u32[]{:S(2)}, u32[]{:S(2)}) async-start(f32[32,1,256]{2,1,0:T(1,128)} %reshape.185), calls=%async_computation.2 | async-start | bytes 65536 | tf_op jit(solution)/shard_map/all_to_all | solution.py:139
  359.5 15.9 %all-to-all-start.3 = ((f32[32,1,256]{2,1,0:T(1,128)}), f32[32,1,256]{2,1,0:T(1,128)S(1)}, u32[]{:S(2)}, u32[]{:S(2)}) async-start(f32[32,1,256]{2,1,0:T(1,128)} %reshape.187), calls=%async_computation.3 | async-start | bytes 65536 | tf_op jit(solution)/shard_map/all_to_all | solution.py:140
  375.5 61.2 %all-to-all-start.1 = ((bf16[2,1024,1024]{2,0,1:T(2,128)(2,1)}), bf16[2,1024,1024]{2,0,1:T(2,128)(2,1)}, u32[]{:S(2)}, u32[]{:S(2)}) async-start(bf16[2,1024,1024]{2,0,1:T(2,128)(2,1)} %copy.121), calls=%async_computation.1 | async-start | bytes 8388608 | tf_op jit(solution)/shard_map/all_to_all | solution.py:142
  436.7 4.6 %copy-start = (f32[32,2,32,1024]{3,2,0,1:T(8,128)S(1)}, f32[32,2,32,1024]{3,2,0,1:T(8,128)}, u32[]{:S(2)}) copy-start(f32[32,2,32,1024]{3,2,0,1:T(8,128)} %mul.174) | copy-start | bytes 25165828
  (6 other events, 9.1 us)
Sparse Core Ops, SparseCore 0:
  11.6 117.4 all-gather.5
  132.7 106.0 all-gather.3
  242.0 50.2 all-gather.7
